TPU v7x, 256 devices: a whole 4x4x8 slice. The times are simulated.
256 devices in a mesh: row: 16 (over y_hi, x, core), col: 16 (over z, y_lo).
Axes of the slice: x: 4, y: 4 (y_hi: 2, y_lo: 2; y = y_hi * 2 + y_lo), z: 8, core: 2. Of those that a mesh axis runs over, the one named last changes fastest.
Arguments:
- inputs: bfloat16 [1024, 16384], P('col', 'row'), may hold values from -6 to 6
- out_grad: bfloat16 [1024, 16384], P('col', 'row'), may hold values from -0.1875 to 0.1875
- states: bfloat16 [16384, 1024], P(('col', 'row')), may hold values from -6 to 6
- in_weight: bfloat16 [16384, 16384], P('row', 'col'), may hold values from -0.046875 to 0.046875
- out_weight: bfloat16 [16384, 16384], P('col', 'row'), may hold values from -0.046875 to 0.046875
- decay_rate: float32 [4, 16384], P(None, ('col', 'row')), may hold values from 0.0015625 to 0.1
- session_ids: int32 [4], replicated, may hold values from 0 to 3, each once
- lengths: int32 [4], replicated, may hold values from 1 to 256, 640 in all
Outputs:
- input_grad: bfloat16 [1024, 16384], P('col', 'row')
- in_weight_grad: bfloat16 [16384, 16384], P('row', 'col')
- out_weight_grad: bfloat16 [16384, 16384], P('col', 'row')
- rate_grad: float32 [4, 16384], P(None, ('col', 'row'))
Inputs may be any that keep to these rules, and one draw needn't show every extreme that they name: `session_ids`: each session appears in exactly one sequence. The lengths sum to 640.
All inputs are finite; a program needn't handle non-finite values.
Results may differ from a plain program's by a relative error of at most 0.024.
Values may be sent and summed in bfloat16 or wider, within the bound.
No kernel may reach another device: no remote copies, remote signals or barrier semaphores. Data moves between devices by JAX's collectives and lax.ppermute only.
A program may use at most 128 MiB of HBM per device.

v0:
```python
import jax
import jax.numpy as jnp
from jax import lax
from jax.sharding import PartitionSpec as P

exact_mode = lax.Precision.HIGHEST


def contract(left_side, right_side, left_dim, right_dim):
    return lax.dot_general(
        left_side,
        right_side,
        (((left_dim,), (right_dim,)), ((), ())),
        preferred_element_type=jnp.float32,
    )


def session_table(session_ids, table_rows):
    return (session_ids[:, None] == jnp.arange(table_rows, dtype=jnp.int32)[None, :]).astype(
        jnp.float32
    )


def gather_rows(share, axis_name, parts):
    spread = jnp.broadcast_to(share[None], (parts,) + share.shape)
    return lax.all_to_all(spread, axis_name, 0, 0).reshape((-1,) + share.shape[1:])


def scatter_sum(partial, axis_name, parts):
    pieces = lax.all_to_all(partial.reshape((parts, -1) + partial.shape[1:]), axis_name, 0, 0)
    return jnp.sum(pieces.astype(jnp.float32), axis=0)


def adjoint_sweep(state_grad, rate_rows, onehot, seq_count):
    channels = state_grad.shape[0]
    seq_rate = jnp.dot(onehot, rate_rows, precision=exact_mode)
    decays = (1.0 - seq_rate).T
    running = state_grad.reshape(channels, seq_count, -1)
    bins = running.shape[2]
    factor = decays[:, :, None]
    shift = 1
    while shift < bins:
        ahead = jnp.concatenate(
            [running[:, :, shift:], jnp.zeros((channels, seq_count, shift), running.dtype)], axis=2
        )
        running = running + factor * ahead
        factor = factor * factor
        shift *= 2
    return running.reshape(channels, -1)


def rate_term(adjoint, states_share, onehot, seq_count):
    channels = adjoint.shape[0]
    adjoint_seq = adjoint.reshape(channels, seq_count, -1)
    previous = states_share.astype(jnp.float32).reshape(channels, seq_count, -1)
    per_seq = jnp.sum(adjoint_seq[:, :, 1:] * previous[:, :, :-1], axis=2)
    return -jnp.dot(onehot.T, per_seq.T, precision=exact_mode)


def per_device(inputs, out_grad, states, in_weight, out_weight, decay_rate, session_ids, lengths):
    n_row = lax.axis_size("row")
    n_col = lax.axis_size("col")
    seq_count = session_ids.shape[0]
    onehot = session_table(session_ids, decay_rate.shape[0])
    grad_rows = gather_rows(out_grad, "col", n_col)
    token_total = grad_rows.shape[0]
    bin_count = token_total // seq_count
    token_ids = jnp.arange(token_total, dtype=jnp.int32)
    seq_match = (token_ids // bin_count)[:, None] == jnp.arange(seq_count, dtype=jnp.int32)[None, :]
    seq_length = jnp.sum(jnp.where(seq_match, lengths[None, :], 0), axis=1)
    valid_bin = token_ids % bin_count >= bin_count - seq_length
    masked = jnp.where(valid_bin[:, None], grad_rows, jnp.zeros_like(grad_rows))
    state_grad = scatter_sum(contract(out_weight, masked, 1, 1).astype(jnp.bfloat16), "row", n_row)
    states_rows = lax.all_gather(states, "row", axis=0, tiled=True)
    out_weight_grad = jnp.dot(states_rows, masked, preferred_element_type=jnp.float32).astype(
        jnp.bfloat16
    )
    adjoint = adjoint_sweep(state_grad, decay_rate, onehot, seq_count)
    rate_grad = rate_term(adjoint, states, onehot, seq_count)
    gathered = gather_rows(adjoint.astype(jnp.bfloat16), "row", n_row)
    input_rows = lax.all_gather(inputs, "col", axis=0, tiled=True)
    in_weight_grad = contract(input_rows, gathered, 0, 1).astype(jnp.bfloat16)
    input_grad = scatter_sum(
        contract(gathered, in_weight, 0, 1).astype(jnp.bfloat16), "col", n_col
    ).astype(jnp.bfloat16)
    return (input_grad, in_weight_grad, out_weight_grad, rate_grad)


def solution(mesh):
    return jax.shard_map(
        per_device,
        mesh=mesh,
        in_specs=(
            P("col", "row"),
            P("col", "row"),
            P(("col", "row"), None),
            P("row", "col"),
            P("col", "row"),
            P(None, ("col", "row")),
            P(),
            P(),
        ),
        out_specs=(P("col", "row"), P("row", "col"), P("col", "row"), P(None, ("col", "row"))),
        check_vma=False,
    )
```

profile of v0, /device:TPU:2, one launch (start us, length us, event | category | flops | bytes accessed | tf_op | source)
XLA Modules:
  0.0 284.3 jit_solution(6921144148416662720)
XLA Ops:
  7.2 2.6 broadcast_in_dim.26
  9.8 9.8 %all-to-all-start = ((bf16[16,64,1024]{2,1,0:T(8,128)(2,1)}), bf16[16,64,1024]{2,1,0:T(8,128)(2,1)}, u32[]{:S(2)}, u32[]{:S(2)}) async-start(bf16[16,64,1024]{2,1,0:T(8,128)(2,1)} %broadcast_in_dim.26), calls=%async_computation | async-start | bytes 4194304 | tf_op jit(solution)/shard_map/all_to_all | solution.py:26
  19.7 50.4 %all-to-all-done = bf16[16,64,1024]{2,1,0:T(8,128)(2,1)} async-done(((bf16[16,64,1024]{2,1,0:T(8,128)(2,1)}), bf16[16,64,1024]{2,1,0:T(8,128)(2,1)}, u32[]{:S(2)}, u32[]{:S(2)}) %all-to-all-start) | async-done | bytes 2097184 | tf_op jit(solution)/shard_map/all_to_all | solution.py:26
  70.1 1.8 bitcast_select_fusion
  72.0 3.7 %convolution_convert_fusion.1 = bf16[1024,1024]{0,1:T(8,128)(2,1)} fusion(bf16[1024,1024]{1,0:T(8,128)(2,1)S(1)} %bitcast_select_fusion, bf16[1024,1024]{1,0:T(8,128)(2,1)S(1)} %copy-done), kind=kOutput, calls=%fused_computation.5 | convolution fusion | flops 2148532224 | bytes 6291456 | tf_op jit(solution)/shard_map/dot_general | solution.py:10
  75.7 7.3 %all-to-all-start.1 = ((bf16[16,64,1024]{2,1,0:T(8,128)(2,1)}), bf16[16,64,1024]{2,1,0:T(8,128)(2,1)}, u32[]{:S(2)}, u32[]{:S(2)}) async-start(bf16[16,64,1024]{2,1,0:T(8,128)(2,1)} %bitcast.25), calls=%async_computation.1 | async-start | bytes 4194304 | tf_op jit(solution)/shard_map/all_to_all | solution.py:30
  83.1 0.7 all-gather.5.cloned.1.call-update
  83.8 0.2 multiply_multiply_fusion
  84.7 28.2 %all-to-all-done.1 = bf16[16,64,1024]{2,1,0:T(8,128)(2,1)} async-done(((bf16[16,64,1024]{2,1,0:T(8,128)(2,1)}), bf16[16,64,1024]{2,1,0:T(8,128)(2,1)}, u32[]{:S(2)}, u32[]{:S(2)}) %all-to-all-start.1) | async-done | bytes 2097184 | tf_op jit(solution)/shard_map/all_to_all | solution.py:30
  112.9 2.0 convert_reduce_fusion
  115.0 0.2 slice.44
  115.2 0.2 multiply_add_fusion.7
  115.4 0.2 slice.45
  115.7 0.2 slice.46
  116.1 0.2 slice.47
  116.4 0.2 slice.48
  116.8 0.2 slice.49
  117.1 0.2 slice.50
  117.7 1.6 broadcast_in_dim.28
  119.3 5.7 %all-to-all-start.2 = ((bf16[16,64,1024]{2,1,0:T(8,128)(2,1)}), bf16[16,64,1024]{2,1,0:T(8,128)(2,1)}, u32[]{:S(2)}, u32[]{:S(2)}) async-start(bf16[16,64,1024]{2,1,0:T(8,128)(2,1)} %broadcast_in_dim.28), calls=%async_computation.2 | async-start | bytes 4194304 | tf_op jit(solution)/shard_map/all_to_all | solution.py:26
  125.0 0.7 all-gather.3.cloned.1.call-update
  125.7 30.0 %all-to-all-done.2 = bf16[16,64,1024]{2,1,0:T(8,128)(2,1)} async-done(((bf16[16,64,1024]{2,1,0:T(8,128)(2,1)}), bf16[16,64,1024]{2,1,0:T(8,128)(2,1)}, u32[]{:S(2)}, u32[]{:S(2)}) %all-to-all-start.2) | async-done | bytes 2097184 | tf_op jit(solution)/shard_map/all_to_all | solution.py:26
  155.7 5.9 %convolution_convert_fusion = bf16[1024,1024]{1,0:T(8,128)(2,1)} fusion(bf16[1024,1024]{1,0:T(8,128)(2,1)} %bitcast.4, bf16[1024,1024]{1,0:T(8,128)(2,1)} %param.11), kind=kOutput, calls=%fused_computation.4 | convolution fusion | flops 2148532224 | bytes 6291456 | tf_op jit(solution)/shard_map/dot_general | solution.py:10
  161.7 4.7 %all-to-all-start.3 = ((bf16[16,64,1024]{2,1,0:T(8,128)(2,1)}), bf16[16,64,1024]{2,1,0:T(8,128)(2,1)}, u32[]{:S(2)}, u32[]{:S(2)}) async-start(bf16[16,64,1024]{2,1,0:T(8,128)(2,1)} %bitcast.26), calls=%async_computation.3 | async-start | bytes 4194304 | tf_op jit(solution)/shard_map/all_to_all | solution.py:30
  166.5 5.9 %convert_bitcast_fusion = bf16[1024,1024]{0,1:T(8,128)(2,1)} fusion(bf16[1024,1024]{1,0:T(8,128)(2,1)} %copy-done.1, bf16[1024,1024]{1,0:T(8,128)(2,1)} %all-gather.5.cloned.1.call-done), kind=kOutput, calls=%fused_computation.2 | convolution fusion | flops 2148532224 | bytes 6291456 | tf_op jit(solution)/shard_map/dot_general | solution.py:75
  172.5 3.9 %copy.31 = bf16[1024,1024]{1,0:T(8,128)(2,1)} copy(bf16[1024,1024]{0,1:T(8,128)(2,1)} %convert_bitcast_fusion) | data formatting | bytes 4194304
  176.4 0.3 fusion.1
  176.7 0.9 convolution_negate_fusion
  177.6 87.4 %all-gather.3.cloned.1.call-done = bf16[1024,1024]{1,0:T(8,128)(2,1)} async-done(((bf16[64,1024]{1,0:T(8,128)(2,1)}), bf16[1024,1024]{1,0:T(8,128)(2,1)}) %all-gather.3.cloned.1.call-update) | async-done | bytes 2097168 | tf_op jit(solution)/shard_map/all_gather | solution.py:81
  265.0 5.9 %convert_bitcast_fusion.1 = bf16[1024,1024]{0,1:T(8,128)(2,1)} fusion(bf16[1024,1024]{1,0:T(8,128)(2,1)} %bitcast.4, bf16[1024,1024]{1,0:T(8,128)(2,1)} %all-gather.3.cloned.1.call-done), kind=kOutput, calls=%fused_computation.3 | convolution fusion | flops 2148532224 | bytes 6291456 | tf_op jit(solution)/shard_map/dot_general | solution.py:10
  270.9 3.9 %copy.30 = bf16[1024,1024]{1,0:T(8,128)(2,1)} copy(bf16[1024,1024]{0,1:T(8,128)(2,1)} %convert_bitcast_fusion.1) | data formatting | bytes 4194304
  274.8 2.7 reduce_sum.41
  (38 shorter events, 2.2 us)
Async XLA Ops:
  7.2 64.8 %copy-start = (bf16[1024,1024]{1,0:T(8,128)(2,1)S(1)}, bf16[1024,1024]{1,0:T(8,128)(2,1)}, u32[]{:S(2)}) copy-start(bf16[1024,1024]{1,0:T(8,128)(2,1)} %param.12) | copy-start | bytes 6291460
  9.8 9.8 %copy-start.3 = (s32[4]{0:T(128)S(1)}, s32[4]{0:T(128)}, u32[]{:S(2)}) copy-start(s32[4]{0:T(128)} %param.15) | copy-start | bytes 52
  9.8 60.3 %all-to-all-start = ((bf16[16,64,1024]{2,1,0:T(8,128)(2,1)}), bf16[16,64,1024]{2,1,0:T(8,128)(2,1)}, u32[]{:S(2)}, u32[]{:S(2)}) async-start(bf16[16,64,1024]{2,1,0:T(8,128)(2,1)} %broadcast_in_dim.26), calls=%async_computation | async-start | bytes 4194304 | tf_op jit(solution)/shard_map/all_to_all | solution.py:26
  72.0 3.7 %copy-start.1 = (bf16[1024,1024]{1,0:T(8,128)(2,1)}, bf16[1024,1024]{1,0:T(8,128)(2,1)S(1)}, u32[]{:S(2)}) copy-start(bf16[1024,1024]{1,0:T(8,128)(2,1)S(1)} %bitcast_select_fusion) | copy-start | bytes 6291460
  75.7 8.1 %copy-start.4 = (f32[4,64]{1,0:T(4,128)S(1)}, f32[4,64]{1,0:T(4,128)}, u32[]{:S(2)}) copy-start(f32[4,64]{1,0:T(4,128)} %param.13) | copy-start | bytes 3076
  75.7 8.1 %copy-start.5 = (s32[4]{0:T(128)S(1)}, s32[4]{0:T(128)}, u32[]{:S(2)}) copy-start(s32[4]{0:T(128)} %param.14) | copy-start | bytes 52
  75.7 37.2 %all-to-all-start.1 = ((bf16[16,64,1024]{2,1,0:T(8,128)(2,1)}), bf16[16,64,1024]{2,1,0:T(8,128)(2,1)}, u32[]{:S(2)}, u32[]{:S(2)}) async-start(bf16[16,64,1024]{2,1,0:T(8,128)(2,1)} %bitcast.25), calls=%async_computation.1 | async-start | bytes 4194304 | tf_op jit(solution)/shard_map/all_to_all | solution.py:30
  83.0 83.5 %all-gather.5.cloned.1.call-start = ((), (), s32[]{:S(2)}) async-start(), calls=%async_computation.5 | async-start | bytes 2228224 | tf_op jit(solution)/shard_map/all_gather | solution.py:74
  119.3 36.5 %all-to-all-start.2 = ((bf16[16,64,1024]{2,1,0:T(8,128)(2,1)}), bf16[16,64,1024]{2,1,0:T(8,128)(2,1)}, u32[]{:S(2)}, u32[]{:S(2)}) async-start(bf16[16,64,1024]{2,1,0:T(8,128)(2,1)} %broadcast_in_dim.28), calls=%async_computation.2 | async-start | bytes 4194304 | tf_op jit(solution)/shard_map/all_to_all | solution.py:26
  125.0 140.0 %all-gather.3.cloned.1.call-start = ((), (), s32[]{:S(2)}) async-start(), calls=%async_computation.4 | async-start | bytes 2228224 | tf_op jit(solution)/shard_map/all_gather | solution.py:81
  161.7 4.8 %copy-start.2 = (bf16[64,1024]{1,0:T(8,128)(2,1)S(1)}, bf16[64,1024]{1,0:T(8,128)(2,1)}, u32[]{:S(2)}) copy-start(bf16[64,1024]{1,0:T(8,128)(2,1)} %param.10) | copy-start | bytes 393220
  161.7 113.1 %all-to-all-start.3 = ((bf16[16,64,1024]{2,1,0:T(8,128)(2,1)}), bf16[16,64,1024]{2,1,0:T(8,128)(2,1)}, u32[]{:S(2)}, u32[]{:S(2)}) async-start(bf16[16,64,1024]{2,1,0:T(8,128)(2,1)} %bitcast.26), calls=%async_computation.3 | async-start | bytes 4194304 | tf_op jit(solution)/shard_map/all_to_all | solution.py:30
Sparse Core Ops, SparseCore 0:
  86.5 76.7 all-gather.4
  165.2 99.7 all-gather.2
where the time goes:
time: 285 us; the launch traced here: 284 us
  waiting for transfers between devices  197 us (69%)
  starting transfers between devices  27.6 us (10%)
  matrix products  22.5 us (8%)
  local copies, waits for them, and re-layouts  14.5 us (5%)
  between operations  14.3 us (5%)
  other arithmetic  8.02 us (3%)
    all_gather x1, waiting for transfers between devices, per_device(): input_rows = lax.all_gather(inputs, 'col', axis=0, tiled=True)  87.4 us
    all_to_all x2, waiting for transfers between devices, gather_rows(): lax.all_to_all(spread, axis_name, 0, 0).reshape((-1,) + share.shape[1:])  80.5 us
    all_to_all x2, waiting for transfers between devices, scatter_sum(): lax.all_to_all(partial.reshape((parts, -1) + partial.shape[1:]), axis_nam...  28.2 us
    dot_general x3, matrix products, contract(): lax.dot_general(left_side, right_side, (((left_dim,), (right_dim,)), ((),...  15.5 us
    all_to_all x2, starting transfers between devices, gather_rows(): lax.all_to_all(spread, axis_name, 0, 0).reshape((-1,) + share.shape[1:])  15.5 us
    all_to_all x2, starting transfers between devices, scatter_sum(): lax.all_to_all(partial.reshape((parts, -1) + partial.shape[1:]), axis_nam...  12.1 us
    unnamed x15, local copies, waits for them, and re-layouts  7.91 us
    dot_general x1, matrix products, per_device(): jnp.dot(states_rows, masked, preferred_element_type=jnp.float32)  5.94 us
  transfers between devices with their start and end apart: 6, of which 4 were waited for; matrix products, arithmetic and copies ran while one was open for 12% of the time, Pallas kernels for 0%

commit v1 on v0

--- a/solution.py
+++ b/solution.py
@@ -78,7 +78,9 @@
     adjoint = adjoint_sweep(state_grad, decay_rate, onehot, seq_count)
     rate_grad = rate_term(adjoint, states, onehot, seq_count)
     gathered = gather_rows(adjoint.astype(jnp.bfloat16), "row", n_row)
-    input_rows = lax.all_gather(inputs, "col", axis=0, tiled=True)
+    input_rows = jnp.concatenate(
+        lax.all_to_all(jnp.stack([inputs] * lax.axis_size("col")), "col", 0, 0), axis=0
+    )
     in_weight_grad = contract(input_rows, gathered, 0, 1).astype(jnp.bfloat16)
     input_grad = scatter_sum(
         contract(gathered, in_weight, 0, 1).astype(jnp.bfloat16), "col", n_col

time: 285 us -> 273 us (0.958)
  waiting for transfers between devices: 197 us -> 154 us
  blocking collectives: 0 us -> 30.8 us
    all_gather x1 -> x0, waiting for transfers between devices: 87.4 us -> none  [per_device(): input_rows = lax.all_gather(inputs, 'col', axis=0, tiled=True)]
    all_to_all x0 -> x1, waiting for transfers between devices: none -> 45.7 us  [per_device(): lax.all_to_all(jnp.stack([inputs] * lax.axis_size('col')), 'col', 0, 0)]
    all_to_all x0 -> x1, blocking collectives: none -> 30.8 us  [gather_rows(): lax.all_to_all(spread, axis_name, 0, 0).reshape((-1,) + share.shape[1:])]
    all_to_all x2 -> x1, waiting for transfers between devices: 80.5 us -> 50.4 us  [gather_rows(): lax.all_to_all(spread, axis_name, 0, 0).reshape((-1,) + share.shape[1:])]
    all_to_all x2, waiting for transfers between devices: 28.2 us -> 50.4 us  [scatter_sum(): lax.all_to_all(partial.reshape((parts, -1) + partial.shape[1:]), axis_nam...]
    all_gather x1, waiting for transfers between devices: 0.02 us -> 6.9 us  [per_device(): states_rows = lax.all_gather(states, 'row', axis=0, tiled=True)]
    all_to_all x2 -> x1, starting transfers between devices: 15.5 us -> 9.76 us  [gather_rows(): lax.all_to_all(spread, axis_name, 0, 0).reshape((-1,) + share.shape[1:])]
    all_to_all x0 -> x1, starting transfers between devices: none -> 4.44 us  [per_device(): lax.all_to_all(jnp.stack([inputs] * lax.axis_size('col')), 'col', 0, 0)]
  transfers between devices with their start and end apart: 6 -> 5, of which waited for: 4 -> 5; matrix products, arithmetic and copies ran while one was open for 12% -> 10% of each run, Pallas kernels for 0% -> 0%
where the time goes in v1:
time: 273 us; the launch traced here: 272 us
  waiting for transfers between devices  154 us (56%)
  blocking collectives  30.8 us (11%)
  starting transfers between devices  27.3 us (10%)
  matrix products  22.6 us (8%)
  local copies, waits for them, and re-layouts  14.7 us (5%)
  between operations  14.3 us (5%)
  other arithmetic  8.02 us (3%)
    all_to_all x1, waiting for transfers between devices, gather_rows(): lax.all_to_all(spread, axis_name, 0, 0).reshape((-1,) + share.shape[1:])  50.4 us
    all_to_all x2, waiting for transfers between devices, scatter_sum(): lax.all_to_all(partial.reshape((parts, -1) + partial.shape[1:]), axis_nam...  50.4 us
    all_to_all x1, waiting for transfers between devices, per_device(): lax.all_to_all(jnp.stack([inputs] * lax.axis_size('col')), 'col', 0, 0)  45.7 us
    all_to_all x1, blocking collectives, gather_rows(): lax.all_to_all(spread, axis_name, 0, 0).reshape((-1,) + share.shape[1:])  30.8 us
    dot_general x3, matrix products, contract(): lax.dot_general(left_side, right_side, (((left_dim,), (right_dim,)), ((),...  15.6 us
    all_to_all x2, starting transfers between devices, scatter_sum(): lax.all_to_all(partial.reshape((parts, -1) + partial.shape[1:]), axis_nam...  13.1 us
    all_to_all x1, starting transfers between devices, gather_rows(): lax.all_to_all(spread, axis_name, 0, 0).reshape((-1,) + share.shape[1:])  9.76 us
    unnamed x17, local copies, waits for them, and re-layouts  7.92 us
  transfers between devices with their start and end apart: 5, of which 5 were waited for; matrix products, arithmetic and copies ran while one was open for 10% of the time, Pallas kernels for 0%

profile of v1, /device:TPU:2, one launch (start us, length us, event | category | flops | bytes accessed | tf_op | source)
XLA Modules:
  0.0 271.8 jit_solution(16994372228694212993)
XLA Ops:
  7.2 2.6 broadcast_in_dim.26
  9.8 9.8 %all-to-all-start = ((bf16[16,64,1024]{2,1,0:T(8,128)(2,1)}), bf16[16,64,1024]{2,1,0:T(8,128)(2,1)}, u32[]{:S(2)}, u32[]{:S(2)}) async-start(bf16[16,64,1024]{2,1,0:T(8,128)(2,1)} %broadcast_in_dim.26), calls=%async_computation | async-start | bytes 4194304 | tf_op jit(solution)/shard_map/all_to_all | solution.py:26
  19.7 50.4 %all-to-all-done = bf16[16,64,1024]{2,1,0:T(8,128)(2,1)} async-done(((bf16[16,64,1024]{2,1,0:T(8,128)(2,1)}), bf16[16,64,1024]{2,1,0:T(8,128)(2,1)}, u32[]{:S(2)}, u32[]{:S(2)}) %all-to-all-start) | async-done | bytes 2097184 | tf_op jit(solution)/shard_map/all_to_all | solution.py:26
  70.1 1.8 bitcast_select_fusion
  72.0 3.7 %convolution_convert_fusion.1 = bf16[1024,1024]{0,1:T(8,128)(2,1)} fusion(bf16[1024,1024]{1,0:T(8,128)(2,1)S(1)} %bitcast_select_fusion, bf16[1024,1024]{1,0:T(8,128)(2,1)S(1)} %copy-done), kind=kOutput, calls=%fused_computation.5 | convolution fusion | flops 2148532224 | bytes 6291456 | tf_op jit(solution)/shard_map/dot_general | solution.py:10
  75.7 7.3 %all-to-all-start.1 = ((bf16[16,64,1024]{2,1,0:T(8,128)(2,1)}), bf16[16,64,1024]{2,1,0:T(8,128)(2,1)}, u32[]{:S(2)}, u32[]{:S(2)}) async-start(bf16[16,64,1024]{2,1,0:T(8,128)(2,1)} %bitcast.28), calls=%async_computation.1 | async-start | bytes 4194304 | tf_op jit(solution)/shard_map/all_to_all | solution.py:30
  84.0 27.7 %all-to-all-done.1 = bf16[16,64,1024]{2,1,0:T(8,128)(2,1)} async-done(((bf16[16,64,1024]{2,1,0:T(8,128)(2,1)}), bf16[16,64,1024]{2,1,0:T(8,128)(2,1)}, u32[]{:S(2)}, u32[]{:S(2)}) %all-to-all-start.1) | async-done | bytes 2097184 | tf_op jit(solution)/shard_map/all_to_all | solution.py:30
  111.7 2.0 convert_reduce_fusion
  113.8 0.2 slice.44
  114.2 0.2 slice.45
  114.5 0.2 slice.46
  114.8 0.2 slice.47
  115.2 0.2 slice.48
  115.5 0.2 slice.49
  115.9 0.2 slice.50
  116.5 0.3 broadcast_in_dim.28
  116.7 30.8 %all_to_all.25 = bf16[16,64,1024]{2,1,0:T(8,128)(2,1)} all-to-all(bf16[16,64,1024]{2,1,0:T(8,128)(2,1)S(1)} %broadcast_in_dim.28), channel_id=1, replica_groups=mesh['row'=16,'col'=16] {'row'}, dimensions={0} | all-to-all | bytes 4194304 | tf_op jit(solution)/shard_map/all_to_all | solution.py:26
  147.5 1.6 stack.2
  149.1 4.4 %all-to-all-start.4 = ((bf16[16,64,1024]{2,1,0:T(8,128)(2,1)}), bf16[16,64,1024]{2,1,0:T(8,128)(2,1)}, u32[]{:S(2)}, u32[]{:S(2)}) async-start(bf16[16,64,1024]{2,1,0:T(8,128)(2,1)} %stack.2), calls=%async_computation.4 | async-start | bytes 4194304 | tf_op jit(solution)/shard_map/all_to_all | solution.py:82
  153.6 0.7 all-gather.2.cloned.1.call-update
  154.3 6.0 %convolution_convert_fusion = bf16[1024,1024]{1,0:T(8,128)(2,1)} fusion(bf16[1024,1024]{1,0:T(8,128)(2,1)} %bitcast.26, bf16[1024,1024]{1,0:T(8,128)(2,1)} %param.11), kind=kOutput, calls=%fused_computation.4 | convolution fusion | flops 2148532224 | bytes 6291456 | tf_op jit(solution)/shard_map/dot_general | solution.py:10
  160.2 45.7 %all-to-all-done.4 = bf16[16,64,1024]{2,1,0:T(8,128)(2,1)} async-done(((bf16[16,64,1024]{2,1,0:T(8,128)(2,1)}), bf16[16,64,1024]{2,1,0:T(8,128)(2,1)}, u32[]{:S(2)}, u32[]{:S(2)}) %all-to-all-start.4) | async-done | bytes 2097184 | tf_op jit(solution)/shard_map/all_to_all | solution.py:82
  205.9 5.8 %all-to-all-start.3 = ((bf16[16,64,1024]{2,1,0:T(8,128)(2,1)}), bf16[16,64,1024]{2,1,0:T(8,128)(2,1)}, u32[]{:S(2)}, u32[]{:S(2)}) async-start(bf16[16,64,1024]{2,1,0:T(8,128)(2,1)} %bitcast.29), calls=%async_computation.3 | async-start | bytes 4194304 | tf_op jit(solution)/shard_map/all_to_all | solution.py:30
  211.8 6.9 %all-gather.2.cloned.1.call-done = bf16[1024,1024]{1,0:T(8,128)(2,1)} async-done(((bf16[64,1024]{1,0:T(8,128)(2,1)}), bf16[1024,1024]{1,0:T(8,128)(2,1)}) %all-gather.2.cloned.1.call-update) | async-done | bytes 2097168 | tf_op jit(solution)/shard_map/all_gather | solution.py:74
  218.7 5.9 %convert_bitcast_fusion = bf16[1024,1024]{0,1:T(8,128)(2,1)} fusion(bf16[1024,1024]{1,0:T(8,128)(2,1)} %copy-done.1, bf16[1024,1024]{1,0:T(8,128)(2,1)} %all-gather.2.cloned.1.call-done), kind=kOutput, calls=%fused_computation.2 | convolution fusion | flops 2148532224 | bytes 6291456 | tf_op jit(solution)/shard_map/dot_general | solution.py:75
  224.6 3.9 %copy.31 = bf16[1024,1024]{1,0:T(8,128)(2,1)} copy(bf16[1024,1024]{0,1:T(8,128)(2,1)} %convert_bitcast_fusion) | data formatting | bytes 4194304
  228.6 0.3 fusion.1
  228.9 0.9 convolution_negate_fusion
  229.7 5.9 %convert_bitcast_fusion.1 = bf16[1024,1024]{0,1:T(8,128)(2,1)} fusion(bf16[1024,1024]{1,0:T(8,128)(2,1)} %bitcast.27, bf16[1024,1024]{1,0:T(8,128)(2,1)} %bitcast.6), kind=kOutput, calls=%fused_computation.3 | convolution fusion | flops 2148532224 | bytes 6291456 | tf_op jit(solution)/shard_map/dot_general | solution.py:10
  235.7 3.9 %copy.30 = bf16[1024,1024]{1,0:T(8,128)(2,1)} copy(bf16[1024,1024]{0,1:T(8,128)(2,1)} %convert_bitcast_fusion.1) | data formatting | bytes 4194304
  239.6 22.7 %all-to-all-done.3 = bf16[16,64,1024]{2,1,0:T(8,128)(2,1)} async-done(((bf16[16,64,1024]{2,1,0:T(8,128)(2,1)}), bf16[16,64,1024]{2,1,0:T(8,128)(2,1)}, u32[]{:S(2)}, u32[]{:S(2)}) %all-to-all-start.3) | async-done | bytes 2097184 | tf_op jit(solution)/shard_map/all_to_all | solution.py:30
  262.3 2.7 reduce_sum.41
  (39 shorter events, 2.5 us)
Async XLA Ops:
  7.2 64.8 %copy-start = (bf16[1024,1024]{1,0:T(8,128)(2,1)S(1)}, bf16[1024,1024]{1,0:T(8,128)(2,1)}, u32[]{:S(2)}) copy-start(bf16[1024,1024]{1,0:T(8,128)(2,1)} %param.12) | copy-start | bytes 6291460
  9.8 9.8 %copy-start.4 = (s32[4]{0:T(128)S(1)}, s32[4]{0:T(128)}, u32[]{:S(2)}) copy-start(s32[4]{0:T(128)} %param.15) | copy-start | bytes 52
  9.8 60.3 %all-to-all-start = ((bf16[16,64,1024]{2,1,0:T(8,128)(2,1)}), bf16[16,64,1024]{2,1,0:T(8,128)(2,1)}, u32[]{:S(2)}, u32[]{:S(2)}) async-start(bf16[16,64,1024]{2,1,0:T(8,128)(2,1)} %broadcast_in_dim.26), calls=%async_computation | async-start | bytes 4194304 | tf_op jit(solution)/shard_map/all_to_all | solution.py:26
  72.0 3.7 %copy-start.1 = (bf16[1024,1024]{1,0:T(8,128)(2,1)}, bf16[1024,1024]{1,0:T(8,128)(2,1)S(1)}, u32[]{:S(2)}) copy-start(bf16[1024,1024]{1,0:T(8,128)(2,1)S(1)} %bitcast_select_fusion) | copy-start | bytes 6291460
  75.7 7.3 %copy-start.5 = (f32[4,64]{1,0:T(4,128)S(1)}, f32[4,64]{1,0:T(4,128)}, u32[]{:S(2)}) copy-start(f32[4,64]{1,0:T(4,128)} %param.13) | copy-start | bytes 3076
  75.7 7.3 %copy-start.6 = (s32[4]{0:T(128)S(1)}, s32[4]{0:T(128)}, u32[]{:S(2)}) copy-start(s32[4]{0:T(128)} %param.14) | copy-start | bytes 52
  75.7 36.0 %all-to-all-start.1 = ((bf16[16,64,1024]{2,1,0:T(8,128)(2,1)}), bf16[16,64,1024]{2,1,0:T(8,128)(2,1)}, u32[]{:S(2)}, u32[]{:S(2)}) async-start(bf16[16,64,1024]{2,1,0:T(8,128)(2,1)} %bitcast.28), calls=%async_computation.1 | async-start | bytes 4194304 | tf_op jit(solution)/shard_map/all_to_all | solution.py:30
  116.7 30.8 %copy-start.3 = (bf16[64,1024]{1,0:T(8,128)(2,1)S(1)}, bf16[64,1024]{1,0:T(8,128)(2,1)}, u32[]{:S(2)}) copy-start(bf16[64,1024]{1,0:T(8,128)(2,1)} %param.8) | copy-start | bytes 393220
  149.1 56.9 %all-to-all-start.4 = ((bf16[16,64,1024]{2,1,0:T(8,128)(2,1)}), bf16[16,64,1024]{2,1,0:T(8,128)(2,1)}, u32[]{:S(2)}, u32[]{:S(2)}) async-start(bf16[16,64,1024]{2,1,0:T(8,128)(2,1)} %stack.2), calls=%async_computation.4 | async-start | bytes 4194304 | tf_op jit(solution)/shard_map/all_to_all | solution.py:82
  153.5 65.2 %all-gather.2.cloned.1.call-start = ((), (), s32[]{:S(2)}) async-start(), calls=%async_computation.5 | async-start | bytes 2228224 | tf_op jit(solution)/shard_map/all_gather | solution.py:74
  205.9 5.8 %copy-start.2 = (bf16[64,1024]{1,0:T(8,128)(2,1)S(1)}, bf16[64,1024]{1,0:T(8,128)(2,1)}, u32[]{:S(2)}) copy-start(bf16[64,1024]{1,0:T(8,128)(2,1)} %param.10) | copy-start | bytes 393220
  205.9 56.3 %all-to-all-start.3 = ((bf16[16,64,1024]{2,1,0:T(8,128)(2,1)}), bf16[16,64,1024]{2,1,0:T(8,128)(2,1)}, u32[]{:S(2)}, u32[]{:S(2)}) async-start(bf16[16,64,1024]{2,1,0:T(8,128)(2,1)} %bitcast.29), calls=%async_computation.3 | async-start | bytes 4194304 | tf_op jit(solution)/shard_map/all_to_all | solution.py:30
Sparse Core Ops, SparseCore 0:
  157.1 61.6 all-gather.1
